TPU v7x, 256 devices: a whole 4x4x8 slice. The times are simulated.
256 devices in a mesh: seq: 64 (over y, z, core), tp: 4 (over x).
Axes of the slice: x: 4, y: 4, z: 8, core: 2. Of those that a mesh axis runs over, the one named last changes fastest.
Arguments:
- tokens: bfloat16 [512, 1152], P('seq'), may hold values from -6 to 6
- attn_gain: float32 [1152], replicated, may hold values from 0.1 to 1.9
- w_query: bfloat16 [1152, 1280], P(None, 'tp'), may hold values from -0.1875 to 0.1875
- w_key: bfloat16 [1152, 384], replicated, may hold values from -0.1875 to 0.1875
- w_value: bfloat16 [1152, 384], replicated, may hold values from -0.1875 to 0.1875
- w_out: bfloat16 [1280, 1152], P('tp'), may hold values from -0.1875 to 0.1875
- prefix_keys: bfloat16 [8, 32768, 384], P(None, 'seq'), may hold values from -92 to 92
- prefix_values: bfloat16 [8, 32768, 384], P(None, 'seq'), may hold values from -6 to 6
- suffix_keys: bfloat16 [512, 128, 384], P('seq'), may hold values from -92 to 92
- suffix_values: bfloat16 [512, 128, 384], P('seq'), may hold values from -6 to 6
- group_of: int32 [512], replicated, may hold values from 0 to 7, as said below
- prefix_len: int32 [8], replicated, may hold values from 1 to 32768, as said below
- suffix_len: int32 [512], replicated, may hold values from 0 to 128, as said below
- mlp_gain: float32 [1152], replicated, may hold values from 0.1 to 1.9
- w_gate: bfloat16 [1152, 3072], P(None, 'tp'), may hold values from -0.1875 to 0.1875
- w_up: bfloat16 [1152, 3072], P(None, 'tp'), may hold values from -0.1875 to 0.1875
- w_down: bfloat16 [3072, 1152], P('tp'), may hold values from -0.109375 to 0.109375
Outputs:
- layer_out: bfloat16 [512, 1152], P('seq')
Inputs may be any that keep to these rules, and one draw needn't show every extreme that they name: `group_of`: prompt group of each request; every request reads its group's stored prefix. `prefix_len`: stored prefix positions in use for each group. `suffix_len`: stored suffix positions in use for each request.
All inputs are finite; a program needn't handle non-finite values.
Results may differ from a plain program's by a relative error of at most 0.018.
Values may be sent and summed in bfloat16 or wider, within the bound.
No kernel may reach another device: no remote copies, remote signals or barrier semaphores. Data moves between devices by JAX's collectives and lax.ppermute only.
A program may use at most 192 MiB of HBM per device.

v0:
```python
import jax
import jax.numpy as jnp
from jax import lax
from jax.sharding import PartitionSpec as P

HEADS = 18
KV_HEADS = 6
HD = 64
NEG_FILL = -1e30


def rms_scale(values_in, gain_row):
    widened = values_in.astype(jnp.float32)
    factor = lax.rsqrt(jnp.mean(widened * widened, axis=-1, keepdims=True) + 1e-05)
    return (widened * factor * gain_row).astype(jnp.bfloat16)


def rotate_heads(blocks, position):
    half_dim = blocks.shape[-1] // 2
    frequency = jnp.power(10000.0, -jnp.arange(half_dim, dtype=jnp.float32) / half_dim)
    angles = position.astype(jnp.float32)[:, None, None] * frequency
    cosine = jnp.cos(angles)
    sine_part = jnp.sin(angles)
    low_half = blocks[..., :half_dim]
    high_half = blocks[..., half_dim:]
    return jnp.concatenate(
        [low_half * cosine - high_half * sine_part, high_half * cosine + low_half * sine_part],
        axis=-1,
    )


def slot_layout(device_tp, tp_count, slot_count):
    per_device = HEADS // tp_count
    surplus = HEADS % tp_count
    start_head = per_device * device_tp + jnp.minimum(device_tp, surplus)
    used_count = per_device + (device_tp < surplus).astype(jnp.int32)
    slot_ids = jnp.arange(slot_count, dtype=jnp.int32)
    head_ids = start_head + slot_ids
    slot_used = (slot_ids < used_count).astype(jnp.float32)
    kv_ids = jnp.minimum(head_ids, HEADS - 1) // (HEADS // KV_HEADS)
    return (kv_ids, slot_used)


def on_device(
    tokens,
    attn_gain,
    w_query,
    w_key,
    w_value,
    w_out,
    prefix_keys,
    prefix_values,
    suffix_keys,
    suffix_values,
    group_of,
    prefix_len,
    suffix_len,
    mlp_gain,
    w_gate,
    w_up,
    w_down,
):
    row_count = tokens.shape[0]
    slot_count = w_query.shape[1] // HD
    group_count = prefix_keys.shape[0]
    prefix_span = prefix_keys.shape[1]
    suffix_span = suffix_keys.shape[1]
    seq_index = lax.axis_index("seq")
    kv_ids, slot_used = slot_layout(lax.axis_index("tp"), lax.axis_size("tp"), slot_count)
    normed = rms_scale(tokens, attn_gain)
    queries = jnp.dot(normed, w_query, preferred_element_type=jnp.float32).reshape(
        row_count, slot_count, HD
    )
    new_keys = jnp.dot(normed, w_key, preferred_element_type=jnp.float32).reshape(
        row_count, KV_HEADS, HD
    )
    new_values = (
        jnp.dot(normed, w_value, preferred_element_type=jnp.float32)
        .astype(jnp.bfloat16)
        .reshape(row_count, KV_HEADS, HD)
    )
    own_start = seq_index * row_count
    own_groups = lax.dynamic_slice_in_dim(group_of, own_start, row_count)
    own_suffix = lax.dynamic_slice_in_dim(suffix_len, own_start, row_count)
    group_ids = jnp.arange(group_count, dtype=jnp.int32)
    own_prefix = jnp.sum(
        jnp.where(own_groups[:, None] == group_ids[None, :], prefix_len[None, :], 0), axis=1
    )
    position = own_prefix + own_suffix
    queries = rotate_heads(queries, position).astype(jnp.bfloat16)
    new_keys = rotate_heads(new_keys, position).astype(jnp.bfloat16)
    every_query = lax.all_gather(
        queries.reshape(row_count, slot_count * HD), "seq", axis=0, tiled=True
    )
    every_query = every_query.reshape(-1, slot_count, HD)
    request_count = every_query.shape[0]
    score_scale = HD ** (-0.5)
    pre_keys = jnp.take(prefix_keys.reshape(group_count, prefix_span, KV_HEADS, HD), kv_ids, axis=2)
    pre_values = jnp.take(
        prefix_values.reshape(group_count, prefix_span, KV_HEADS, HD), kv_ids, axis=2
    )
    pre_scores = (
        jnp.einsum("rsd,gpsd->rsgp", every_query, pre_keys, preferred_element_type=jnp.float32)
        * score_scale
    )
    pre_spots = seq_index * prefix_span + jnp.arange(prefix_span, dtype=jnp.int32)
    group_match = group_of[:, None] == group_ids[None, :]
    length_match = pre_spots[None, :] < prefix_len[:, None]
    pre_live = group_match[:, None, :, None] & length_match[None, None, :, :]
    top_score = jnp.max(
        jnp.where(pre_live, pre_scores, NEG_FILL).reshape(request_count, slot_count, -1), axis=2
    )
    pre_weights = jnp.where(pre_live, jnp.exp(pre_scores - top_score[:, :, None, None]), 0.0)
    totals = jnp.sum(pre_weights, axis=(2, 3))
    mixed_sum = jnp.einsum(
        "rsgp,gpsd->rsd",
        pre_weights.astype(jnp.bfloat16),
        pre_values,
        preferred_element_type=jnp.float32,
    )
    gathered = (
        lax.all_to_all(top_score[None], "seq", split_axis=1, concat_axis=0, tiled=True),
        lax.all_to_all(totals[None], "seq", split_axis=1, concat_axis=0, tiled=True),
        lax.all_to_all(mixed_sum[None], "seq", split_axis=1, concat_axis=0, tiled=True),
    )
    part_top = jnp.max(gathered[0], axis=0)
    part_scale = jnp.exp(gathered[0] - part_top[None])
    part_total = jnp.sum(part_scale * gathered[1], axis=0)
    part_mixed = jnp.sum(part_scale[..., None] * gathered[2], axis=0)
    suf_keys = jnp.take(suffix_keys.reshape(row_count, suffix_span, KV_HEADS, HD), kv_ids, axis=2)
    suf_values = jnp.take(
        suffix_values.reshape(row_count, suffix_span, KV_HEADS, HD), kv_ids, axis=2
    )
    suf_scores = (
        jnp.einsum("rsd,rjsd->rsj", queries, suf_keys, preferred_element_type=jnp.float32)
        * score_scale
    )
    suf_live = (jnp.arange(suffix_span, dtype=jnp.int32)[None, :] < own_suffix[:, None])[:, None, :]
    suf_top = jnp.max(jnp.where(suf_live, suf_scores, NEG_FILL), axis=2)
    own_keys = jnp.take(new_keys, kv_ids, axis=1).astype(jnp.float32)
    own_values = jnp.take(new_values, kv_ids, axis=1).astype(jnp.float32)
    own_score = jnp.sum(queries.astype(jnp.float32) * own_keys, axis=-1) * score_scale
    final_top = jnp.maximum(jnp.maximum(part_top, suf_top), own_score)
    carried = jnp.exp(part_top - final_top)
    suf_weights = jnp.where(suf_live, jnp.exp(suf_scores - final_top[:, :, None]), 0.0)
    own_weight = jnp.exp(own_score - final_top)
    denominator = carried * part_total + jnp.sum(suf_weights, axis=2) + own_weight
    own_low = lax.optimization_barrier(own_weight.astype(jnp.bfloat16)).astype(jnp.float32)
    numerator = carried[..., None] * part_mixed + own_low[..., None] * own_values
    numerator = numerator + jnp.einsum(
        "rsj,rjsd->rsd",
        suf_weights.astype(jnp.bfloat16),
        suf_values,
        preferred_element_type=jnp.float32,
    )
    attended = (numerator / denominator[..., None] * slot_used[None, :, None]).astype(jnp.bfloat16)
    head_part = jnp.dot(
        attended.reshape(row_count, slot_count * HD), w_out, preferred_element_type=jnp.float32
    )
    head_total = lax.psum(head_part.astype(jnp.bfloat16), "tp").astype(jnp.float32)
    hidden = (tokens.astype(jnp.float32) + head_total).astype(jnp.bfloat16)
    mlp_in = rms_scale(hidden, mlp_gain)
    gate_part = jnp.dot(mlp_in, w_gate, preferred_element_type=jnp.float32)
    up_part = jnp.dot(mlp_in, w_up, preferred_element_type=jnp.float32)
    activation = (jax.nn.silu(gate_part) * up_part).astype(jnp.bfloat16)
    down_part = jnp.dot(activation, w_down, preferred_element_type=jnp.float32)
    down_total = lax.psum(down_part.astype(jnp.bfloat16), "tp").astype(jnp.float32)
    return (hidden.astype(jnp.float32) + down_total).astype(jnp.bfloat16)


def solution(mesh):
    return jax.shard_map(
        on_device,
        mesh=mesh,
        in_specs=(
            P("seq", None),
            P(),
            P(None, "tp"),
            P(),
            P(),
            P("tp", None),
            P(None, "seq", None),
            P(None, "seq", None),
            P("seq", None, None),
            P("seq", None, None),
            P(),
            P(),
            P(),
            P(),
            P(None, "tp"),
            P(None, "tp"),
            P("tp", None),
        ),
        out_specs=P("seq", None),
        check_vma=False,
    )
```

profile of v0, /device:TPU:32, one launch (start us, length us, event | category | flops | bytes accessed | tf_op | source)
XLA Modules:
  0.0 266.4 jit_solution(10958488884695363522)
XLA Ops:
  0.0 0.8 iota_compare_fusion
  0.8 0.8 dynamic_slice.6
  1.6 0.8 fusion.28
  2.5 0.6 compare_and_fusion
  3.1 0.8 select_reduce_fusion.1
  3.9 0.7 broadcast_compare_fusion
  4.6 1.4 fusion.61
  6.1 1.5 fusion.63
  7.6 0.1 reshape.264
  7.9 0.8 add_convert_fusion.1
  8.7 0.1 multiply_cosine_fusion
  8.9 0.6 gather_fusion.2
  9.5 0.2 multiply_reduce_fusion.1
  9.6 0.1 convert_element_type.88
  9.7 50.4 %all_gather.3 = bf16[512,320]{1,0:T(8,128)(2,1)S(1)} all-gather(bf16[8,320]{1,0:T(8,128)(2,1)S(1)} %convert_element_type.88), channel_id=1, replica_groups=mesh['seq'=64,'tp'=4] {'seq'}, dimensions={0}, use_global_device_ids=true | all-gather | bytes 332800 | tf_op jit(solution)/shard_map/all_gather | solution.py:92
  60.1 0.2 copy.86
  60.3 4.7 %copy.81 = bf16[8,512,384]{1,2,0:T(8,128)(2,1)} copy(bf16[8,512,384]{2,1,0:T(8,128)(2,1)} %param.29) | data formatting | bytes 6291456 | tf_op args[6]
  65.0 3.9 %copy.82 = bf16[8,512,6,64]{1,3,0,2:T(8,128)(2,1)} copy(bf16[8,512,6,64]{1,3,2,0:T(8,128)(2,1)} %bitcast.92) | data formatting | bytes 6291456 | tf_op jit(solution)/shard_map/reshape | solution.py:98
  68.9 4.3 %gather_fusion = bf16[5,8,512,64]{2,3,1,0:T(8,128)(2,1)} fusion(bf16[8,512,6,64]{1,3,0,2:T(8,128)(2,1)} %copy.82, s32[1024]{0:T(1024)S(1)} %pad_clamp_fusion), kind=kCustom, calls=%fused_computation.clone | custom fusion | bytes 5242900 | tf_op jit(solution)/shard_map/jit(_take)/gather | solution.py:98
  73.1 2.1 broadcast_and_fusion
  75.2 19.6 %fusion = (f32[512,5]{0,1:T(8,128)S(1)}, f32[5,8,512,512]{3,2,1,0:T(8,128)}) fusion(pred[512,8,512]{0,2,1:T(8,128)(4,1)} %broadcast_and_fusion, bf16[512,5,64,1]{0,2,3,1:T(8,128)(2,1)S(1)} %bitcast.100, bf16[5,8,512,64]{2,3,1,0:T(8,128)(2,1)} %gather_fusion, pred[5]{0:T(512)(128)(4,1)S(1)} %get-tuple-element.36), kind=kOutput, calls=%fused_computation.8 | convolution fusion | flops 1374942720 | bytes 46999556 | tf_op jit(solution)/shard_map/rsd,gpsd->rsgp/dot_general | solution.py:103
  94.8 0.9 copy.87
  95.6 8.0 %all-to-all-start = ((f32[1,512,5]{2,0,1:T(1,128)}), f32[1,512,5]{2,0,1:T(1,128)S(1)}, u32[]{:S(2)}, u32[]{:S(2)}) async-start(f32[1,512,5]{2,0,1:T(1,128)} %copy.87), calls=%async_computation | async-start | bytes 524288 | tf_op jit(solution)/shard_map/all_to_all | solution.py:122
  103.7 1.5 copy.89
  105.2 0.7 gather_fusion.1
  105.9 2.3 copy.98
  108.2 1.8 gather_fusion.5
  110.0 4.7 %copy.92 = bf16[8,512,384]{1,2,0:T(8,128)(2,1)} copy(bf16[8,512,384]{2,1,0:T(8,128)(2,1)} %param.30) | data formatting | bytes 6291456 | tf_op args[7]
  114.7 3.9 %copy.93 = bf16[8,512,6,64]{1,3,0,2:T(8,128)(2,1)} copy(bf16[8,512,6,64]{1,3,2,0:T(8,128)(2,1)} %bitcast.93) | data formatting | bytes 6291456 | tf_op jit(solution)/shard_map/reshape | solution.py:100
  118.6 4.3 %gather_fusion.3 = bf16[5,8,512,64]{2,3,1,0:T(8,128)(2,1)} fusion(bf16[8,512,6,64]{1,3,0,2:T(8,128)(2,1)} %copy.93, s32[1024]{0:T(1024)S(1)} %pad_clamp_fusion), kind=kCustom, calls=%fused_computation.3.clone | custom fusion | bytes 5242900 | tf_op jit(solution)/shard_map/jit(_take)/gather | solution.py:99
  122.9 18.8 %fusion.3 = f32[512,5]{0,1:T(8,128)S(1)} fusion(f32[5,8,512,512]{3,2,1,0:T(8,128)} %get-tuple-element.35, f32[512,5]{0,1:T(8,128)S(1)} %get-tuple-element.34, pred[512,8,512]{0,2,1:T(8,128)(4,1)} %broadcast_and_fusion), kind=kLoop, calls=%fused_computation.11 | loop fusion | flops 41940480 | bytes 44060672 | tf_op jit(solution)/shard_map/reduce_sum | solution.py:114
  141.7 16.7 %fusion.18 = f32[1,512,5,64]{1,3,2,0:T(8,128)} fusion(f32[5,8,512,512]{3,2,1,0:T(8,128)} %get-tuple-element.35, f32[512,5]{0,1:T(8,128)S(1)} %get-tuple-element.34, pred[512,8,512]{0,2,1:T(8,128)(4,1)S(1)} %copy-done.2, bf16[5,8,512,64]{2,3,1,0:T(8,128)(2,1)S(1)} %copy-done.1, pred[5]{0:T(512)(128)(4,1)S(1)} %get-tuple-element.36), kind=kOutput, calls=%fused_computation.29 | convolution fusion | flops 1385431040 | bytes 47327236 | tf_op jit(solution)/shard_map/rsgp,gpsd->rsd/dot_general | solution.py:115
  158.5 1.3 select_bitcast_fusion.1
  159.8 0.2 convolution_convert_fusion.2
  160.0 0.9 copy.99
  160.9 10.5 %all-to-all-start.2 = ((f32[1,512,5]{2,0,1:T(1,128)}), f32[1,512,5]{2,0,1:T(1,128)}, u32[]{:S(2)}, u32[]{:S(2)}) async-start(f32[1,512,5]{2,0,1:T(1,128)} %copy.99), calls=%async_computation.2 | async-start | bytes 524288 | tf_op jit(solution)/shard_map/all_to_all | solution.py:123
  171.4 1.4 fusion.26
  172.8 0.1 reshape.266
  172.9 0.6 gather_fusion.4
  173.5 2.4 copy.95
  175.9 0.5 broadcast.335
  176.4 5.9 %reduce.1 = f32[512,5,64]{2,1,0:T(8,128)} reduce(f32[512,5,1,64]{3,2,1,0:T(1,128)S(1)} %bitcast.96, f32[]{:T(128)} %broadcast.335), dimensions={2}, to_apply=%bitcast.79.reduce_sub_computation | reduce | bytes 1310724
  182.4 3.1 %reshape.341 = f32[64,1,2560]{2,1,0:T(1,128)} reshape(f32[512,5,64]{2,1,0:T(8,128)} %reduce.1) | data formatting | bytes 1310720
  185.5 10.5 %all-to-all-start.1 = ((f32[64,1,2560]{2,1,0:T(1,128)}), f32[64,1,2560]{2,1,0:T(1,128)S(1)}, u32[]{:S(2)}, u32[]{:S(2)}) async-start(f32[64,1,2560]{2,1,0:T(1,128)} %reshape.341), calls=%async_computation.1 | async-start | bytes 1310720 | tf_op jit(solution)/shard_map/all_to_all | solution.py:124
  196.2 0.5 copy.111
  196.9 0.6 convert_element_type.93
  197.5 1.5 copy.112
  199.0 0.2 fusion.46
  199.2 0.6 add_add_fusion
  199.8 2.1 fusion.24
  201.9 14.0 %all-to-all-done.1 = f32[64,1,2560]{2,1,0:T(1,128)S(1)} async-done(((f32[64,1,2560]{2,1,0:T(1,128)}), f32[64,1,2560]{2,1,0:T(1,128)S(1)}, u32[]{:S(2)}, u32[]{:S(2)}) %all-to-all-start.1) | async-done | bytes 655392 | tf_op jit(solution)/shard_map/all_to_all | solution.py:124
  215.9 3.1 %reduce.2 = f32[64,2560]{1,0:T(8,128)} reduce(f32[64,1,2560]{2,1,0:T(1,128)S(1)} %all-to-all-done.1, f32[]{:T(128)} %broadcast.335), dimensions={1}, to_apply=%all_to_all.14.reduce_sub_computation | reduce | bytes 1310724 | tf_op jit(solution)/shard_map/all_to_all | solution.py:124
  219.1 2.7 %reshape.342 = f32[512,5,1,64]{3,2,1,0:T(1,128)S(1)} reshape(f32[64,2560]{1,0:T(8,128)} %reduce.2) | data formatting | bytes 1310720
  221.8 0.4 fusion.15
  222.2 1.0 fusion.43
  223.2 0.7 reshape.268
  223.9 2.0 convolution_convert_fusion.1
  225.9 18.2 %psum.14 = bf16[8,1152]{1,0:T(8,128)(2,1)} all-reduce(bf16[8,1152]{1,0:T(8,128)(2,1)} %convolution_convert_fusion.1), channel_id=1, replica_groups=mesh['seq'=64,'tp'=4] {'tp'}, use_global_device_ids=true, to_apply=%region_10.14 | all-reduce | flops 9216 | bytes 36864 | tf_op jit(solution)/shard_map/psum | solution.py:160
  244.1 0.9 fusion.32
  245.0 0.6 copy-done.6
  245.6 2.5 fusion.53
  248.1 2.1 convolution_convert_fusion
  250.2 14.9 %psum.15 = bf16[8,1152]{1,0:T(8,128)(2,1)S(1)} all-reduce(bf16[8,1152]{1,0:T(8,128)(2,1)} %convolution_convert_fusion), channel_id=1, replica_groups=mesh['seq'=64,'tp'=4] {'tp'}, use_global_device_ids=true, to_apply=%region_12.16 | all-reduce | flops 9216 | bytes 36864 | tf_op jit(solution)/shard_map/psum | solution.py:167
  265.1 1.3 fusion.35
  (42 shorter events, 0.9 us)
Async XLA Ops:
  0.0 248.1 %copy-start = (bf16[768,1152]{1,0:T(8,128)(2,1)S(1)}, bf16[768,1152]{1,0:T(8,128)(2,1)}, u32[]{:S(2)}) copy-start(bf16[768,1152]{1,0:T(8,128)(2,1)} %param.39) | copy-start | bytes 5308420
  3.1 155.4 %copy-start.9 = (pred[5]{0:T(512)(128)(4,1)}, pred[5]{0:T(512)(128)(4,1)S(1)}, u32[]{:S(2)}) copy-start(pred[5]{0:T(512)(128)(4,1)S(1)} %get-tuple-element.36) | copy-start | bytes 19
  95.6 65.3 %all-to-all-start = ((f32[1,512,5]{2,0,1:T(1,128)}), f32[1,512,5]{2,0,1:T(1,128)S(1)}, u32[]{:S(2)}, u32[]{:S(2)}) async-start(f32[1,512,5]{2,0,1:T(1,128)} %copy.87), calls=%async_computation | async-start | bytes 524288 | tf_op jit(solution)/shard_map/all_to_all | solution.py:122
  122.9 18.8 %copy-start.1 = (bf16[5,8,512,64]{2,3,1,0:T(8,128)(2,1)S(1)}, bf16[5,8,512,64]{2,3,1,0:T(8,128)(2,1)}, u32[]{:S(2)}) copy-start(bf16[5,8,512,64]{2,3,1,0:T(8,128)(2,1)} %gather_fusion.3) | copy-start | bytes 7864324
  122.9 18.8 %copy-start.2 = (pred[512,8,512]{0,2,1:T(8,128)(4,1)S(1)}, pred[512,8,512]{0,2,1:T(8,128)(4,1)}, u32[]{:S(2)}) copy-start(pred[512,8,512]{0,2,1:T(8,128)(4,1)} %broadcast_and_fusion) | copy-start | bytes 6291460
  158.4 1.3 copy-start.4
  158.5 1.3 copy-start.5
  158.5 1.3 copy-start.7
  160.9 24.6 %all-to-all-start.2 = ((f32[1,512,5]{2,0,1:T(1,128)}), f32[1,512,5]{2,0,1:T(1,128)}, u32[]{:S(2)}, u32[]{:S(2)}) async-start(f32[1,512,5]{2,0,1:T(1,128)} %copy.99), calls=%async_computation.2 | async-start | bytes 524288 | tf_op jit(solution)/shard_map/all_to_all | solution.py:123
  185.5 30.5 %all-to-all-start.1 = ((f32[64,1,2560]{2,1,0:T(1,128)}), f32[64,1,2560]{2,1,0:T(1,128)S(1)}, u32[]{:S(2)}, u32[]{:S(2)}) async-start(f32[64,1,2560]{2,1,0:T(1,128)} %reshape.341), calls=%async_computation.1 | async-start | bytes 1310720 | tf_op jit(solution)/shard_map/all_to_all | solution.py:124
  222.2 25.8 %copy-start.3 = (bf16[1152,768]{1,0:T(8,128)(2,1)S(1)}, bf16[1152,768]{1,0:T(8,128)(2,1)}, u32[]{:S(2)}) copy-start(bf16[1152,768]{1,0:T(8,128)(2,1)} %param.38) | copy-start | bytes 5308420
  223.9 24.2 %copy-start.8 = (f32[1152]{0:T(1024)S(1)}, f32[1152]{0:T(1024)}, u32[]{:S(2)}) copy-start(f32[1152]{0:T(1024)} %param.36) | copy-start | bytes 13828
  245.0 0.6 copy-start.6
where the time goes:
time: 268 us; the launch traced here: 266 us
  blocking collectives  83.5 us (31%)
  matrix products  49.5 us (18%)
  local copies, waits for them, and re-layouts  48.6 us (18%)
  other arithmetic  41.5 us (15%)
  starting transfers between devices  29.1 us (11%)
  waiting for transfers between devices  14 us (5%)
    all_gather x1, blocking collectives, on_device(): lax.all_gather(queries.reshape(row_count, slot_count * HD), 'seq', axis=0...  50.4 us
    unnamed x28, local copies, waits for them, and re-layouts  20.3 us
    dot_general x1, matrix products, on_device(): jnp.einsum('rsd,gpsd->rsgp', every_query, pre_keys, preferred_element_typ...  19.6 us
    reduce_sum x1, other arithmetic, on_device(): totals = jnp.sum(pre_weights, axis=(2, 3))  18.8 us
    psum x1, blocking collectives, on_device(): lax.psum(head_part.astype(jnp.bfloat16), 'tp').astype(jnp.float32)  18.2 us
    dot_general x1, matrix products, on_device(): jnp.einsum('rsgp,gpsd->rsd', pre_weights.astype(jnp.bfloat16), pre_values...  16.7 us
    psum x1, blocking collectives, on_device(): lax.psum(down_part.astype(jnp.bfloat16), 'tp').astype(jnp.float32)  14.9 us
    all_to_all x1, waiting for transfers between devices, on_device(): lax.all_to_all(mixed_sum[None], 'seq', split_axis=1, concat_axis=0, tiled...  14 us
  transfers between devices with their start and end apart: 3, of which 1 were waited for; matrix products, arithmetic and copies ran while one was open for 29% of the time, Pallas kernels for 0%

commit v1 on v0

--- a/solution.py
+++ b/solution.py
@@ -7,6 +7,12 @@
 KV_HEADS = 6
 HD = 64
 NEG_FILL = -1e30
+
+
+def swap_blocks(x, name, split, join):
+    cells = jnp.split(x, lax.axis_size(name), axis=split)
+    received = lax.all_to_all(jnp.stack(cells), name, 0, 0)
+    return jnp.concatenate(received, axis=join)
 
 
 def rms_scale(values_in, gain_row):
@@ -120,7 +126,7 @@
     )
     gathered = (
         lax.all_to_all(top_score[None], "seq", split_axis=1, concat_axis=0, tiled=True),
-        lax.all_to_all(totals[None], "seq", split_axis=1, concat_axis=0, tiled=True),
+        swap_blocks(totals[None], "seq", 1, 0),
         lax.all_to_all(mixed_sum[None], "seq", split_axis=1, concat_axis=0, tiled=True),
     )
     part_top = jnp.max(gathered[0], axis=0)

time: 268 us -> 270 us (level)
    unnamed x28 -> x36, local copies, waits for them, and re-layouts: 20.3 us -> 20.2 us
  transfers between devices with their start and end apart: 3 -> 3, of which waited for: 1 -> 1; matrix products, arithmetic and copies ran while one was open for 29% -> 22% of each run, Pallas kernels for 0% -> 0%
where the time goes in v1:
time: 270 us; the launch traced here: 269 us
  blocking collectives  83.5 us (31%)
  matrix products  51.6 us (19%)
  local copies, waits for them, and re-layouts  48.1 us (18%)
  other arithmetic  41 us (15%)
  starting transfers between devices  28.7 us (11%)
  waiting for transfers between devices  15.4 us (6%)
    all_gather x1, blocking collectives, on_device(): lax.all_gather(queries.reshape(row_count, slot_count * HD), 'seq', axis=0...  50.4 us
    unnamed x36, local copies, waits for them, and re-layouts  20.2 us
    dot_general x1, matrix products, on_device(): jnp.einsum('rsd,gpsd->rsgp', every_query, pre_keys, preferred_element_typ...  19.6 us
    dot_general x1, matrix products, on_device(): jnp.einsum('rsgp,gpsd->rsd', pre_weights.astype(jnp.bfloat16), pre_values...  18.8 us
    psum x1, blocking collectives, on_device(): lax.psum(head_part.astype(jnp.bfloat16), 'tp').astype(jnp.float32)  18.2 us
    reduce_sum x1, other arithmetic, on_device(): totals = jnp.sum(pre_weights, axis=(2, 3))  18.1 us
    all_to_all x1, waiting for transfers between devices, on_device(): lax.all_to_all(mixed_sum[None], 'seq', split_axis=1, concat_axis=0, tiled...  15.4 us
    psum x1, blocking collectives, on_device(): lax.psum(down_part.astype(jnp.bfloat16), 'tp').astype(jnp.float32)  14.9 us
  transfers between devices with their start and end apart: 3, of which 1 were waited for; matrix products, arithmetic and copies ran while one was open for 22% of the time, Pallas kernels for 0%

profile of v1, /device:TPU:32, one launch (start us, length us, event | category | flops | bytes accessed | tf_op | source)
XLA Modules:
  0.0 268.7 jit_solution(12710181129257673156)
XLA Ops:
  0.0 0.8 iota_compare_fusion
  0.8 0.8 dynamic_slice.6
  1.6 0.8 fusion.29
  2.5 0.5 compare_and_fusion
  3.0 0.8 select_reduce_fusion.1
  3.9 0.7 broadcast_compare_fusion
  4.6 1.4 fusion.62
  6.0 1.5 fusion.64
  7.9 1.2 add_convert_fusion.1
  9.1 0.1 multiply_cosine_fusion
  9.3 0.6 gather_fusion.2
  9.9 0.2 multiply_reduce_fusion
  10.2 50.4 %all_gather.3 = bf16[512,320]{1,0:T(8,128)(2,1)S(1)} all-gather(bf16[8,320]{1,0:T(8,128)(2,1)S(1)} %convert_element_type.88), channel_id=1, replica_groups=mesh['seq'=64,'tp'=4] {'seq'}, dimensions={0}, use_global_device_ids=true | all-gather | bytes 332800 | tf_op jit(solution)/shard_map/all_gather | solution.py:98
  60.5 0.2 copy.218
  60.7 4.7 %copy.213 = bf16[8,512,384]{1,2,0:T(8,128)(2,1)} copy(bf16[8,512,384]{2,1,0:T(8,128)(2,1)} %param.29) | data formatting | bytes 6291456 | tf_op args[6]
  65.4 3.9 %copy.214 = bf16[8,512,6,64]{1,3,0,2:T(8,128)(2,1)} copy(bf16[8,512,6,64]{1,3,2,0:T(8,128)(2,1)} %bitcast.224) | data formatting | bytes 6291456 | tf_op jit(solution)/shard_map/reshape | solution.py:104
  69.3 4.3 %gather_fusion = bf16[5,8,512,64]{2,3,1,0:T(8,128)(2,1)} fusion(bf16[8,512,6,64]{1,3,0,2:T(8,128)(2,1)} %copy.214, s32[1024]{0:T(1024)S(1)} %pad_clamp_fusion), kind=kCustom, calls=%fused_computation.clone | custom fusion | bytes 5242900 | tf_op jit(solution)/shard_map/jit(_take)/gather | solution.py:104
  73.6 2.1 broadcast_and_fusion
  75.6 19.6 %fusion = (f32[512,5]{0,1:T(8,128)S(1)}, f32[5,8,512,512]{3,2,1,0:T(8,128)}) fusion(pred[512,8,512]{0,2,1:T(8,128)(4,1)} %broadcast_and_fusion, bf16[512,5,64,1]{0,2,3,1:T(8,128)(2,1)S(1)} %bitcast.232, bf16[5,8,512,64]{2,3,1,0:T(8,128)(2,1)} %gather_fusion, pred[5]{0:T(512)(128)(4,1)S(1)} %get-tuple-element.100), kind=kOutput, calls=%fused_computation.8 | convolution fusion | flops 1374942720 | bytes 46999556 | tf_op jit(solution)/shard_map/rsd,gpsd->rsgp/dot_general | solution.py:109
  95.2 18.1 %fusion.3 = f32[512,5]{0,1:T(8,128)S(1)} fusion(f32[5,8,512,512]{3,2,1,0:T(8,128)} %get-tuple-element.99, f32[512,5]{0,1:T(8,128)S(1)} %get-tuple-element.98, pred[512,8,512]{0,2,1:T(8,128)(4,1)} %broadcast_and_fusion), kind=kLoop, calls=%fused_computation.11 | loop fusion | flops 41940480 | bytes 44060672 | tf_op jit(solution)/shard_map/reduce_sum | solution.py:120
  113.4 0.2 slice_bitcast_fusion.38
  113.6 0.2 slice_bitcast_fusion
  113.7 0.2 slice_bitcast_fusion.19
  113.9 0.3 stack.259
  114.3 0.8 copy.231
  115.1 8.0 %all-to-all-start.2 = ((f32[64,1,8,5]{2,1,3,0:T(1,128)}), f32[64,1,8,5]{2,1,3,0:T(1,128)S(1)}, u32[]{:S(2)}, u32[]{:S(2)}) async-start(f32[64,1,8,5]{2,1,3,0:T(1,128)} %copy.231), calls=%async_computation.2 | async-start | bytes 327680 | tf_op jit(solution)/shard_map/all_to_all | solution.py:14
  123.1 1.5 copy.221
  124.6 0.7 gather_fusion.1
  125.3 2.3 copy.230
  127.6 1.8 gather_fusion.5
  129.5 4.7 %copy.224 = bf16[8,512,384]{1,2,0:T(8,128)(2,1)} copy(bf16[8,512,384]{2,1,0:T(8,128)(2,1)} %param.30) | data formatting | bytes 6291456 | tf_op args[7]
  134.1 3.9 %copy.225 = bf16[8,512,6,64]{1,3,0,2:T(8,128)(2,1)} copy(bf16[8,512,6,64]{1,3,2,0:T(8,128)(2,1)} %bitcast.225) | data formatting | bytes 6291456 | tf_op jit(solution)/shard_map/reshape | solution.py:106
  138.1 4.3 %gather_fusion.3 = bf16[5,8,512,64]{2,3,1,0:T(8,128)(2,1)} fusion(bf16[8,512,6,64]{1,3,0,2:T(8,128)(2,1)} %copy.225, s32[1024]{0:T(1024)S(1)} %pad_clamp_fusion), kind=kCustom, calls=%fused_computation.3.clone | custom fusion | bytes 5242900 | tf_op jit(solution)/shard_map/jit(_take)/gather | solution.py:105
  142.4 18.8 %fusion.18 = f32[1,512,5,64]{1,3,2,0:T(8,128)} fusion(f32[5,8,512,512]{3,2,1,0:T(8,128)} %get-tuple-element.99, f32[512,5]{0,1:T(8,128)S(1)} %get-tuple-element.98, pred[512,8,512]{0,2,1:T(8,128)(4,1)} %broadcast_and_fusion, bf16[5,8,512,64]{2,3,1,0:T(8,128)(2,1)} %gather_fusion.3, pred[5]{0:T(512)(128)(4,1)S(1)} %copy-done.10), kind=kOutput, calls=%fused_computation.29 | convolution fusion | flops 1385431040 | bytes 47327236 | tf_op jit(solution)/shard_map/rsgp,gpsd->rsd/dot_general | solution.py:121
  161.2 1.3 select_bitcast_fusion.1
  162.4 0.2 convolution_convert_fusion.2
  162.7 0.9 copy.219
  163.6 10.3 %all-to-all-start = ((f32[1,512,5]{2,0,1:T(1,128)}), f32[1,512,5]{2,0,1:T(1,128)S(1)}, u32[]{:S(2)}, u32[]{:S(2)}) async-start(f32[1,512,5]{2,0,1:T(1,128)} %copy.219), calls=%async_computation | async-start | bytes 524288 | tf_op jit(solution)/shard_map/all_to_all | solution.py:128
  173.9 1.4 fusion.26
  175.4 0.7 gather_fusion.4
  176.1 2.4 copy.227
  178.5 0.5 broadcast.329
  179.0 5.9 %reduce.1 = f32[512,5,64]{2,1,0:T(8,128)} reduce(f32[512,5,1,64]{3,2,1,0:T(1,128)S(1)} %bitcast.228, f32[]{:T(128)} %broadcast.329), dimensions={2}, to_apply=%bitcast.211.reduce_sub_computation | reduce | bytes 1310724
  184.9 3.1 %reshape.339 = f32[64,1,2560]{2,1,0:T(1,128)} reshape(f32[512,5,64]{2,1,0:T(8,128)} %reduce.1) | data formatting | bytes 1310720
  188.0 10.3 %all-to-all-start.1 = ((f32[64,1,2560]{2,1,0:T(1,128)}), f32[64,1,2560]{2,1,0:T(1,128)S(1)}, u32[]{:S(2)}, u32[]{:S(2)}) async-start(f32[64,1,2560]{2,1,0:T(1,128)} %reshape.339), calls=%async_computation.1 | async-start | bytes 1310720 | tf_op jit(solution)/shard_map/all_to_all | solution.py:130
  198.5 0.5 copy.243
  199.2 0.6 convert_element_type.93
  199.8 0.2 fusion.47
  200.0 0.6 add_add_fusion
  200.6 2.1 fusion.24
  202.8 15.4 %all-to-all-done.1 = f32[64,1,2560]{2,1,0:T(1,128)S(1)} async-done(((f32[64,1,2560]{2,1,0:T(1,128)}), f32[64,1,2560]{2,1,0:T(1,128)S(1)}, u32[]{:S(2)}, u32[]{:S(2)}) %all-to-all-start.1) | async-done | bytes 655392 | tf_op jit(solution)/shard_map/all_to_all | solution.py:130
  218.2 3.1 %reduce.2 = f32[64,2560]{1,0:T(8,128)} reduce(f32[64,1,2560]{2,1,0:T(1,128)S(1)} %all-to-all-done.1, f32[]{:T(128)} %broadcast.329), dimensions={1}, to_apply=%all_to_all.23.reduce_sub_computation | reduce | bytes 1310724 | tf_op jit(solution)/shard_map/all_to_all | solution.py:130
  221.3 2.7 %reshape.340 = f32[512,5,1,64]{3,2,1,0:T(1,128)S(1)} reshape(f32[64,2560]{1,0:T(8,128)} %reduce.2) | data formatting | bytes 1310720
  224.0 0.4 fusion.15
  224.5 1.0 fusion.44
  225.4 0.7 reshape.266
  226.1 2.0 convolution_convert_fusion.1
  228.1 18.2 %psum.14 = bf16[8,1152]{1,0:T(8,128)(2,1)} all-reduce(bf16[8,1152]{1,0:T(8,128)(2,1)} %convolution_convert_fusion.1), channel_id=1, replica_groups=mesh['seq'=64,'tp'=4] {'tp'}, use_global_device_ids=true, to_apply=%region_10.14 | all-reduce | flops 9216 | bytes 36864 | tf_op jit(solution)/shard_map/psum | solution.py:166
  246.3 0.9 fusion.33
  247.2 0.6 copy-done.4
  247.8 2.5 fusion.54
  250.3 2.1 convolution_convert_fusion
  252.4 14.9 %psum.15 = bf16[8,1152]{1,0:T(8,128)(2,1)S(1)} all-reduce(bf16[8,1152]{1,0:T(8,128)(2,1)} %convolution_convert_fusion), channel_id=1, replica_groups=mesh['seq'=64,'tp'=4] {'tp'}, use_global_device_ids=true, to_apply=%region_12.16 | all-reduce | flops 9216 | bytes 36864 | tf_op jit(solution)/shard_map/psum | solution.py:173
  267.3 1.3 fusion.36
  (55 shorter events, 1.2 us)
Async XLA Ops:
  0.0 250.3 %copy-start = (bf16[768,1152]{1,0:T(8,128)(2,1)S(1)}, bf16[768,1152]{1,0:T(8,128)(2,1)}, u32[]{:S(2)}) copy-start(bf16[768,1152]{1,0:T(8,128)(2,1)} %param.39) | copy-start | bytes 5308420
  2.4 5.1 %copy-start.11 = (f32[8]{0:T(128)}, f32[8]{0:T(128)S(1)}, u32[]{:S(2)}) copy-start(f32[8]{0:T(128)S(1)} %add_rsqrt_fusion.1) | copy-start | bytes 100
  3.0 72.6 %copy-start.9 = (pred[5]{0:T(512)(128)(4,1)}, pred[5]{0:T(512)(128)(4,1)S(1)}, u32[]{:S(2)}) copy-start(pred[5]{0:T(512)(128)(4,1)S(1)} %get-tuple-element.100) | copy-start | bytes 19
  4.6 133.5 %copy-start.8 = (s32[1024]{0:T(1024)}, s32[1024]{0:T(1024)S(1)}, u32[]{:S(2)}) copy-start(s32[1024]{0:T(1024)S(1)} %pad_clamp_fusion) | copy-start | bytes 12292
  115.1 48.5 %all-to-all-start.2 = ((f32[64,1,8,5]{2,1,3,0:T(1,128)}), f32[64,1,8,5]{2,1,3,0:T(1,128)S(1)}, u32[]{:S(2)}, u32[]{:S(2)}) async-start(f32[64,1,8,5]{2,1,3,0:T(1,128)} %copy.231), calls=%async_computation.2 | async-start | bytes 327680 | tf_op jit(solution)/shard_map/all_to_all | solution.py:14
  138.0 4.3 %copy-start.10 = (pred[5]{0:T(512)(128)(4,1)S(1)}, pred[5]{0:T(512)(128)(4,1)}, u32[]{:S(2)}) copy-start(pred[5]{0:T(512)(128)(4,1)} %copy-done.9) | copy-start | bytes 19
  161.1 1.3 copy-start.2
  161.1 1.3 copy-start.3
  161.1 1.3 copy-start.5
  161.2 1.3 copy-start.12
  163.6 24.4 %all-to-all-start = ((f32[1,512,5]{2,0,1:T(1,128)}), f32[1,512,5]{2,0,1:T(1,128)S(1)}, u32[]{:S(2)}, u32[]{:S(2)}) async-start(f32[1,512,5]{2,0,1:T(1,128)} %copy.219), calls=%async_computation | async-start | bytes 524288 | tf_op jit(solution)/shard_map/all_to_all | solution.py:128
  184.9 13.4 %copy-start.13 = (s32[8]{0:T(128)S(1)}, s32[8]{0:T(128)}, u32[]{:S(2)}) copy-start(s32[8]{0:T(128)} %get-tuple-element.19) | copy-start | bytes 100
  188.0 30.2 %all-to-all-start.1 = ((f32[64,1,2560]{2,1,0:T(1,128)}), f32[64,1,2560]{2,1,0:T(1,128)S(1)}, u32[]{:S(2)}, u32[]{:S(2)}) async-start(f32[64,1,2560]{2,1,0:T(1,128)} %reshape.339), calls=%async_computation.1 | async-start | bytes 1310720 | tf_op jit(solution)/shard_map/all_to_all | solution.py:130
  200.6 23.8 %copy-start.7 = (f32[8,5]{0,1:T(8,128)S(1)}, f32[8,5]{0,1:T(8,128)}, u32[]{:S(2)}) copy-start(f32[8,5]{0,1:T(8,128)} %get-tuple-element.12) | copy-start | bytes 484
  224.4 25.8 %copy-start.1 = (bf16[1152,768]{1,0:T(8,128)(2,1)S(1)}, bf16[1152,768]{1,0:T(8,128)(2,1)}, u32[]{:S(2)}) copy-start(bf16[1152,768]{1,0:T(8,128)(2,1)} %param.38) | copy-start | bytes 5308420
  226.1 24.2 %copy-start.6 = (f32[1152]{0:T(1024)S(1)}, f32[1152]{0:T(1024)}, u32[]{:S(2)}) copy-start(f32[1152]{0:T(1024)} %param.36) | copy-start | bytes 13828
  247.2 0.6 copy-start.4
